TPU v7x, 128 devices: a whole 4x4x4 slice. The times are simulated.
128 devices in a mesh: dp: 8 (over x_hi, z), tensor: 16 (over y, x_lo, core).
Axes of the slice: x: 4 (x_hi: 2, x_lo: 2; x = x_hi * 2 + x_lo), y: 4, z: 4, core: 2. Of those that a mesh axis runs over, the one named last changes fastest.
Arguments:
- tokens: bfloat16 [16384, 2048], P(('dp', 'tensor')), parts along dimension 0, may hold values from -6 to 6
- segment_ids: int32 [16384], P('dp'), parts along dimension 0, may hold values from 0 to 3, never falling along the last dimension, each value on 1 to 1024 neighbouring positions
- attention_gain: float32 [2048], replicated, may hold values from 0.1 to 1.9
- query_weight: bfloat16 [2048, 2048], P(None, 'tensor'), may hold values from -1 to 1
- key_weight: bfloat16 [2048, 2048], P(None, 'tensor'), may hold values from -1 to 1
- value_weight: bfloat16 [2048, 2048], P(None, 'tensor'), may hold values from -0.125 to 0.125
- output_weight: bfloat16 [2048, 2048], P('tensor'), may hold values from -0.125 to 0.125
- ffn_gain: float32 [2048], replicated, may hold values from 0.1 to 1.9
- shared_gate: bfloat16 [2048, 2816], P(None, 'tensor'), may hold values from -0.125 to 0.125
- shared_up: bfloat16 [2048, 2816], P(None, 'tensor'), may hold values from -0.125 to 0.125
- shared_down: bfloat16 [2816, 2048], P('tensor'), may hold values from -0.109375 to 0.109375
- expert_gate: bfloat16 [16, 2048, 1408], P('tensor'), may hold values from -0.125 to 0.125
- expert_up: bfloat16 [16, 2048, 1408], P('tensor'), may hold values from -0.125 to 0.125
- expert_down: bfloat16 [16, 1408, 2048], P('tensor'), may hold values from -0.15625 to 0.15625
- expert_ids: int32 [16384, 6], P('dp'), parts along dimension 0, may hold values from 0 to 15, all different within a row; in each aligned block of 128 rows (0 to 127, 128 to 255, ...) at most 64 rows name the same one
- gate_weights: float32 [16384, 6], P('dp'), parts along dimension 0, may hold values from 0.05 to 0.35
- page_table: int32 [128], P('dp'), parts along dimension 0, may hold values from 0 to 15, each once
Outputs:
- layer_out: bfloat16 [16384, 2048], P(('dp', 'tensor')), parts along dimension 0
- kv_pages: bfloat16 [2, 128, 128, 2048], P(None, 'dp', None, 'tensor'), parts along dimension 1
There are 8 independent parts, one for each index of `dp`. A program takes and returns all parts, laid end to end along the dimension named above; an argument that names none is the same for every part. Nothing has to cross between parts.
Inputs may be any that keep to these rules, and one draw needn't show every extreme that they name: `segment_ids`: ids never fall along the stream; each of the 4 prompts holds 1 to 1024 tokens and one holds exactly 1024. `expert_ids`: each row names 6 different experts; within each aligned block of 128 rows (the tokens of one index of tensor) no expert is named by more than 64 rows, a bound that some block reaches. `page_table`: each cache page is named once.
All inputs are finite; a program needn't handle non-finite values.
Results may differ from a plain program's by a relative error of at most 0.02.
The roundings to bfloat16 on the way count: a program that leaves them out, or rounds other values in their place, can miss the bound.
Values may be sent and summed in bfloat16 or wider, within the bound.
No kernel may reach another device: no remote copies, remote signals or barrier semaphores. Data moves between devices by JAX's collectives and lax.ppermute only.
A program may use at most 128 MiB of HBM per device.

v0:
```python
import jax
import jax.numpy as jnp
from jax import lax
from jax.sharding import PartitionSpec as P

HD = 128
TOP = 6
PAGE = 128


def rms_scale(hidden, gain):
    widened = hidden.astype(jnp.float32)
    inverse = lax.rsqrt(jnp.mean(widened * widened, axis=-1, keepdims=True) + 1e-06)
    return (widened * inverse * gain).astype(jnp.bfloat16)


def attend(projected, segment_ids, head_count):
    total_tokens = projected.shape[0]
    inner = head_count * HD
    queries = projected[:, :inner].reshape(total_tokens, head_count, HD)
    keys = projected[:, inner : 2 * inner].reshape(total_tokens, head_count, HD)
    values = projected[:, 2 * inner :].reshape(total_tokens, head_count, HD)
    scale = HD ** (-0.5)
    positions = jnp.arange(total_tokens, dtype=jnp.int32)
    span = min(512, total_tokens)

    def one_block(start):
        query_rows = lax.dynamic_slice_in_dim(queries, start, span, 0)
        query_segments = lax.dynamic_slice_in_dim(segment_ids, start, span, 0)
        query_positions = start + jnp.arange(span, dtype=jnp.int32)
        scores = (
            jnp.einsum("qhd,khd->hqk", query_rows, keys, preferred_element_type=jnp.float32) * scale
        )
        allowed = (query_segments[:, None] == segment_ids[None, :]) & (
            positions[None, :] <= query_positions[:, None]
        )
        scores = jnp.where(allowed[None], scores, -jnp.inf)
        highest = jnp.max(scores, axis=-1, keepdims=True)
        weights = jnp.exp(scores - highest)
        probs = (weights / jnp.sum(weights, axis=-1, keepdims=True)).astype(jnp.bfloat16)
        context = jnp.einsum("hqk,khd->qhd", probs, values, preferred_element_type=jnp.float32)
        return context.astype(jnp.bfloat16)

    starts = jnp.arange(total_tokens // span, dtype=jnp.int32) * span
    context = lax.map(one_block, starts).reshape(total_tokens, inner)
    return (context, keys.reshape(total_tokens, inner), values.reshape(total_tokens, inner))


def slot_tables(block_ids, block_gates, expert_count, capacity):
    row_count = block_ids.shape[0]
    labels = jnp.arange(expert_count, dtype=jnp.int32)
    match = (block_ids[:, :, None] == labels[None, None, :]).astype(jnp.int32)
    hits = jnp.sum(match, axis=1)
    before = jnp.cumsum(hits, axis=0) - hits
    rank = jnp.sum(match * before[:, None, :], axis=2)
    flat = (block_ids * capacity + rank).reshape(-1)
    owner = jnp.broadcast_to(jnp.arange(row_count, dtype=jnp.int32)[:, None], block_ids.shape)
    slot_token = jnp.zeros((expert_count * capacity,), jnp.int32).at[flat].set(owner.reshape(-1))
    slot_weight = (
        jnp.zeros((expert_count * capacity,), jnp.float32).at[flat].set(block_gates.reshape(-1))
    )
    return (slot_token, slot_weight)


def expert_apply(incoming, expert_gate, expert_up, expert_down):
    gate_part = jnp.einsum(
        "secd,edf->secf", incoming, expert_gate, preferred_element_type=jnp.float32
    )
    upward = jnp.einsum("secd,edf->secf", incoming, expert_up, preferred_element_type=jnp.float32)
    hidden = (jax.nn.silu(gate_part) * upward).astype(jnp.bfloat16)
    produced = jnp.einsum("secf,efd->secd", hidden, expert_down, preferred_element_type=jnp.float32)
    return produced.astype(jnp.bfloat16)


def shards(
    tokens,
    segment_ids,
    attention_gain,
    query_weight,
    key_weight,
    value_weight,
    output_weight,
    ffn_gain,
    shared_gate,
    shared_up,
    shared_down,
    expert_gate,
    expert_up,
    expert_down,
    expert_ids,
    gate_weights,
    page_table,
):
    tok_dev = tokens.shape[0]
    groups = lax.axis_size("tensor")
    position = lax.axis_index("tensor")
    inner = query_weight.shape[1]
    head_count = inner // HD
    projection = jnp.concatenate([query_weight, key_weight, value_weight], axis=1)
    projected = jnp.dot(
        rms_scale(lax.all_gather(tokens, "tensor", axis=0, tiled=True), attention_gain),
        projection,
        preferred_element_type=jnp.float32,
    ).astype(jnp.bfloat16)
    context, keys, values = attend(projected, segment_ids, head_count)
    cache = jnp.stack([keys, values]).reshape(2, -1, PAGE, inner)
    kv_pages = jnp.zeros_like(cache).at[:, page_table].set(cache)
    attention = lax.psum_scatter(
        jnp.dot(context, output_weight, preferred_element_type=jnp.float32).astype(jnp.bfloat16),
        "tensor",
        scatter_dimension=0,
        tiled=True,
    ).astype(jnp.float32)
    residual = (tokens.astype(jnp.float32) + attention).astype(jnp.bfloat16)
    normed_ffn = rms_scale(residual, ffn_gain)
    shared_columns = jnp.concatenate([shared_gate, shared_up], axis=1)
    shared_width = shared_gate.shape[1]
    local_experts = expert_gate.shape[0]
    expert_count = local_experts * groups
    capacity = tok_dev * TOP // expert_count + tok_dev // 8
    id_blocks = expert_ids.reshape(groups, tok_dev, -1)
    gate_blocks = gate_weights.reshape(groups, tok_dev, -1)

    def block_table(id_block, gate_block):
        return slot_tables(id_block, gate_block, expert_count, capacity)

    all_tokens, all_weights = jax.vmap(block_table)(id_blocks, gate_blocks)
    all_tokens = all_tokens.reshape(groups, expert_count, capacity)
    all_weights = all_weights.reshape(groups, expert_count, capacity)
    chosen_slots = lax.dynamic_slice_in_dim(all_tokens, position * local_experts, local_experts, 1)
    chosen_weights = lax.dynamic_slice_in_dim(
        all_weights, position * local_experts, local_experts, 1
    )
    offsets = (jnp.arange(groups, dtype=jnp.int32) * tok_dev)[:, None, None]
    stream_slots = (chosen_slots + offsets).reshape(-1)
    joined = jnp.dot(
        lax.all_gather(normed_ffn, "tensor", axis=0, tiled=True),
        shared_columns,
        preferred_element_type=jnp.float32,
    )
    hidden_all = (jax.nn.silu(joined[:, :shared_width]) * joined[:, shared_width:]).astype(
        jnp.bfloat16
    )
    own_slots = all_tokens[position]
    outgoing = normed_ffn[own_slots.reshape(-1)].reshape(groups, local_experts, capacity, -1)
    produced = expert_apply(
        lax.all_to_all(outgoing, "tensor", split_axis=0, concat_axis=0, tiled=True),
        expert_gate,
        expert_up,
        expert_down,
    )
    term = jnp.dot(hidden_all, shared_down, preferred_element_type=jnp.float32)
    model_width = term.shape[1]
    weighted = chosen_weights.reshape(-1, 1) * produced.reshape(-1, model_width).astype(jnp.float32)
    term = term.at[stream_slots].add(weighted)
    ffn_out = lax.psum_scatter(
        term.astype(jnp.bfloat16), "tensor", scatter_dimension=0, tiled=True
    ).astype(jnp.float32)
    layer_out = (residual.astype(jnp.float32) + ffn_out).astype(jnp.bfloat16)
    return (layer_out, kv_pages)


def solution(mesh):
    placed = (
        P(("dp", "tensor"), None),
        P("dp"),
        P(),
        P(None, "tensor"),
        P(None, "tensor"),
        P(None, "tensor"),
        P("tensor", None),
        P(),
        P(None, "tensor"),
        P(None, "tensor"),
        P("tensor", None),
        P("tensor", None, None),
        P("tensor", None, None),
        P("tensor", None, None),
        P("dp", None),
        P("dp", None),
        P("dp"),
    )
    return jax.shard_map(
        shards,
        mesh=mesh,
        in_specs=placed,
        out_specs=(P(("dp", "tensor"), None), P(None, "dp", None, "tensor")),
        check_vma=False,
    )
```

profile of v0, /device:TPU:0, one launch (start us, length us, event | category | flops | bytes accessed | tf_op | source)
XLA Modules:
  0.0 538.0 jit_solution(10992776695320439391)
XLA Ops:
  8.0 56.3 %all-gather.3.cloned.1.call-done = bf16[2048,2048]{1,0:T(8,128)(2,1)} async-done(((bf16[128,2048]{1,0:T(8,128)(2,1)}), bf16[2048,2048]{1,0:T(8,128)(2,1)}) %all-gather.3.cloned.1.call-update) | async-done | bytes 8388624 | tf_op jit(solution)/shard_map/all_gather | solution.py:101
  64.3 5.2 fusion.13
  70.1 6.0 %fusion.44 = bf16[2048,384]{1,0:T(8,128)(2,1)S(1)} fusion(bf16[2048,2048]{1,0:T(8,128)(2,1)S(1)} %copy-done.2, f32[2048]{0:T(1024)S(1)} %copy-done.13, f32[2048]{0:T(1024)S(1)} %add_rsqrt_fusion, bf16[2048,128]{1,0:T(8,128)(2,1)S(1)} %copy-done.12, bf16[2048,128]{1,0:T(8,128)(2,1)} %param.23, bf16[2048,128]{1,0:T(8,128)(2,1)} %param.22), kind=kOutput, calls=%fused_computation.51 | convolution fusion | flops 3243507712 | bytes 11550720 | tf_op jit(solution)/shard_map/dot_general | solution.py:100
  77.3 25.8 %while.11 = (s32[]{:T(128)}, bf16[4,512,1,128]{3,1,2,0:T(8,128)(2,1)S(1)}, s32[4]{0:T(128)S(1)}, s32[2048]{0:T(1024)S(1)}, bf16[2048,1,128]{2,0,1:T(8,128)(2,1)S...) while((s32[]{:T(128)}, ...), condition=%wide.region_4.5_spmd.clone, body=%wide.region_1.4_spmd.clone.sunk | while | flops 548470272 | bytes 13922475 | solution.py:45
  103.0 6.6 %convolution_convert_fusion = bf16[2048,2048]{1,0:T(8,128)(2,1)} fusion(bf16[2048,128]{1,0:T(8,128)(2,1)S(1)} %bitcast.144, bf16[128,2048]{1,0:T(8,128)(2,1)} %param.25), kind=kOutput, calls=%fused_computation.32 | convolution fusion | flops 1077936128 | bytes 9437184 | tf_op jit(solution)/shard_map/dot_general | solution.py:109
  110.2 98.4 %reduce-scatter.3.cloned.1.call-done = bf16[128,2048]{1,0:T(8,128)(2,1)} async-done(((bf16[2048,2048]{1,0:T(8,128)(2,1)}), bf16[128,2048]{1,0:T(8,128)(2,1)}) %reduce-scatter.3.cloned.1.call-update) | async-done | bytes 524304 | tf_op jit(solution)/shard_map/reduce_scatter | solution.py:108
  209.9 2.0 fusion.63
  214.1 1.7 mul.116
  215.8 23.3 %fusion.78 = s32[16,128,16]{2,0,1:T(8,128)S(1)} fusion(s32[16,128,16]{2,0,1:T(8,128)S(1)} %copy.43), kind=kOutput, calls=%fused_computation.107 | output fusion | flops 4161536 | bytes 262144 | tf_op jit(solution)/shard_map/vmap(jit(cumsum))/reduce_window_sum | solution.py:54
  240.2 1.6 copy.45
  242.7 45.4 %scatter_custom_fusion.2 = s32[16384]{0:T(1024)S(1)} fusion(s32[12288]{0:T(1024)S(1)} %reshape.275, s32[12288]{0:T(1024)S(1)} %reshape.277, s32[]{:T(128)} %constant.27.clone.1), kind=kCustom, calls=%fused_computation.84 | custom fusion | bytes 65540
  288.4 6.1 %gather_fusion = bf16[1024,2048]{1,0:T(8,128)(2,1)} fusion(bf16[128,2048]{1,0:T(8,128)(2,1)S(1)} %copy-done.1, s32[1024]{0:T(1024)S(1)} %broadcast_clamp_fusion), kind=kCustom, calls=%fused_computation | custom fusion | bytes 8392704 | tf_op jit(solution)/shard_map/gather | solution.py:145
  294.4 4.7 all-to-all-start
  300.4 45.6 %scatter_custom_fusion.3 = f32[16384]{0:T(1024)S(1)} fusion(s32[12288]{0:T(1024)S(1)} %reshape.275, f32[12288]{0:T(1024)S(1)} %reshape.283, f32[]{:T(128)} %constant.9.clone.1), kind=kCustom, calls=%fused_computation.82 | custom fusion | bytes 65540
  346.2 3.3 all-to-all-done
  349.5 11.7 %fusion.24 = f32[16,64,1408]{2,1,0:T(8,128)} fusion(bf16[1,2048,1408]{2,1,0:T(8,128)(2,1)} %param.31, bf16[16,1,64,2048]{3,2,1,0:T(8,128)(2,1)} %all-to-all-done), kind=kOutput, calls=%fused_computation.37 | convolution fusion | flops 5905580032 | bytes 15728640 | tf_op jit(solution)/shard_map/secd,edf->secf/dot_general | solution.py:69
  361.2 21.0 %fusion.36 = bf16[16,64,2048]{2,1,0:T(8,128)(2,1)} fusion(bf16[1,1408,2048]{2,1,0:T(8,128)(2,1)} %param.32, f32[16,64,1408]{2,1,0:T(8,128)} %fusion.24, bf16[1,2048,1408]{2,1,0:T(8,128)(2,1)} %param.30, bf16[16,1,64,2048]{3,2,1,0:T(8,128)(2,1)} %all-to-all-done), kind=kOutput, calls=%fused_computation.49 | convolution fusion | flops 11821907968 | bytes 25690112 | tf_op jit(solution)/shard_map/secf,efd->secd/dot_general | solution.py:71
  382.2 5.8 %fusion.57 = f32[2048,352]{0,1:T(8,128)S(1)} fusion(bf16[2048,2048]{1,0:T(8,128)(2,1)} %all-gather.5.cloned.1.call-done, bf16[2048,176]{0,1:T(8,128)(2,1)S(1)} %copy-done.11, bf16[2048,176]{0,1:T(8,128)(2,1)} %param.27), kind=kOutput, calls=%fused_computation.62 | convolution fusion | flops 2955673600 | bytes 12713984 | tf_op jit(solution)/shard_map/dot_general | solution.py:136
  388.0 8.1 %fusion.65 = f32[2048,2048]{1,0:T(8,128)} fusion(bf16[176,2048]{1,0:T(8,128)(2,1)S(1)} %copy-done, f32[2048,352]{0,1:T(8,128)S(1)} %fusion.57), kind=kOutput, calls=%fused_computation.75 | convolution fusion | flops 1478557696 | bytes 20381696 | tf_op jit(solution)/shard_map/dot_general | solution.py:152
  396.1 26.5 %scatter_custom_fusion = f32[2048,2048]{1,0:T(8,128)} fusion(f32[2048,2048]{1,0:T(8,128)} %fusion.65, s32[1024]{0:T(1024)S(1)} %bitcast.148, bf16[1024,2048]{1,0:T(8,128)(2,1)} %bitcast.141, f32[1024]{0:T(1024)S(1)} %mul.120), kind=kCustom, calls=%fused_computation.29 | custom fusion | flops 6291456 | bytes 20975616 | tf_op jit(solution)/shard_map/scatter-add | solution.py:155
  422.7 9.1 %convert_element_type.101 = bf16[2048,2048]{1,0:T(8,128)(2,1)} convert(f32[2048,2048]{1,0:T(8,128)} %scatter_custom_fusion) | non-fusion elementwise | flops 4194304 | bytes 25165824 | tf_op jit(solution)/shard_map/convert_element_type | solution.py:157
  434.8 3.0 scatter_fusion
  437.8 91.4 %reduce-scatter.5.cloned.1.call-done = bf16[128,2048]{1,0:T(8,128)(2,1)} async-done(((bf16[2048,2048]{1,0:T(8,128)(2,1)}), bf16[128,2048]{1,0:T(8,128)(2,1)}) %reduce-scatter.5.cloned.1.call-update) | async-done | bytes 524304 | tf_op jit(solution)/shard_map/reduce_scatter | solution.py:156
  529.2 2.1 fusion.64
  (105 shorter events, 30.4 us)
Async XLA Ops:
  7.2 380.8 %copy-start = (bf16[176,2048]{1,0:T(8,128)(2,1)S(1)}, bf16[176,2048]{1,0:T(8,128)(2,1)}, u32[]{:S(2)}) copy-start(bf16[176,2048]{1,0:T(8,128)(2,1)} %param.29) | copy-start | bytes 2162692
  7.2 57.1 %all-gather.3.cloned.1.call-start = ((), (), s32[]{:S(2)}) async-start(), calls=%async_computation.3 | async-start | bytes 8912896 | tf_op jit(solution)/shard_map/all_gather | solution.py:101
  7.2 62.3 %copy-start.12 = (bf16[2048,128]{1,0:T(8,128)(2,1)S(1)}, bf16[2048,128]{1,0:T(8,128)(2,1)}, u32[]{:S(2)}) copy-start(bf16[2048,128]{1,0:T(8,128)(2,1)} %param.24) | copy-start | bytes 1572868
  7.9 200.7 %reduce-scatter.3.cloned.1.call-start = ((), (), s32[]{:S(2)}) async-start(), calls=%async_computation.4 | async-start | bytes 8912896 | tf_op jit(solution)/shard_map/reduce_scatter | solution.py:108
  8.0 61.6 %copy-start.13 = (f32[2048]{0:T(1024)S(1)}, f32[2048]{0:T(1024)}, u32[]{:S(2)}) copy-start(f32[2048]{0:T(1024)} %param.21) | copy-start | bytes 24580
  64.3 5.8 %copy-start.2 = (bf16[2048,2048]{1,0:T(8,128)(2,1)S(1)}, bf16[2048,2048]{1,0:T(8,128)(2,1)}, u32[]{:S(2)}) copy-start(bf16[2048,2048]{1,0:T(8,128)(2,1)} %all-gather.3.cloned.1.call-done) | copy-start | bytes 25165828
  76.1 1.2 copy-start.7
  109.6 98.9 %copy-start.3 = (bf16[128,2048]{1,0:T(8,128)(2,1)S(1)}, bf16[128,2048]{1,0:T(8,128)(2,1)}, u32[]{:S(2)}) copy-start(bf16[128,2048]{1,0:T(8,128)(2,1)} %param.19) | copy-start | bytes 1572868
  109.6 100.3 %copy-start.8 = (f32[2048]{0:T(1024)S(1)}, f32[2048]{0:T(1024)}, u32[]{:S(2)}) copy-start(f32[2048]{0:T(1024)} %param.26) | copy-start | bytes 24580
  109.6 102.5 %copy-start.5 = (s32[2048,6]{0,1:T(8,128)S(1)}, s32[2048,6]{0,1:T(8,128)}, u32[]{:S(2)}) copy-start(s32[2048,6]{0,1:T(8,128)} %param.33) | copy-start | bytes 147460
  109.7 272.5 %all-gather.5.cloned.1.call-start = ((), (), s32[]{:S(2)}) async-start(), calls=%async_computation.5 | async-start | bytes 8912896 | tf_op jit(solution)/shard_map/all_gather | solution.py:137
  215.8 26.8 %copy-start.10 = (s32[2]{0:T(128)S(1)}, s32[2]{0:T(128)}, u32[]{:S(2)}) copy-start(s32[2]{0:T(128)} %constant.41) | copy-start | bytes 28
  215.8 26.8 %copy-start.9 = (s32[2]{0:T(128)S(1)}, s32[2]{0:T(128)}, u32[]{:S(2)}) copy-start(s32[2]{0:T(128)} %constant.69) | copy-start | bytes 28
  239.1 49.3 %copy-start.1 = (bf16[128,2048]{1,0:T(8,128)(2,1)S(1)}, bf16[128,2048]{1,0:T(8,128)(2,1)}, u32[]{:S(2)}) copy-start(bf16[128,2048]{1,0:T(8,128)(2,1)} %fusion.63) | copy-start | bytes 1572868
  294.4 4.9 copy-start.6
  294.4 55.0 %all-to-all-start = ((bf16[16,1,64,2048]{3,2,1,0:T(8,128)(2,1)}), bf16[16,1,64,2048]{3,2,1,0:T(8,128)(2,1)}, u32[]{:S(2)}, u32[]{:S(2)}) async-start(bf16[16,1,64,2048]{3,2,1,0:T(8,128)(2,1)} %bitcast.140), calls=%async_computation.1 | async-start | bytes 8388608 | tf_op jit(solution)/shard_map/all_to_all | solution.py:147
  299.1 230.1 %reduce-scatter.5.cloned.1.call-start = ((), (), s32[]{:S(2)}) async-start(), calls=%async_computation.6 | async-start | bytes 8912896 | tf_op jit(solution)/shard_map/reduce_scatter | solution.py:156
  361.2 21.0 %copy-start.11 = (bf16[2048,176]{0,1:T(8,128)(2,1)S(1)}, bf16[2048,176]{0,1:T(8,128)(2,1)}, u32[]{:S(2)}) copy-start(bf16[2048,176]{0,1:T(8,128)(2,1)} %param.28) | copy-start | bytes 2162692
  431.7 0.7 copy-start.14
  432.4 96.8 %copy-start.4 = (bf16[128,2048]{1,0:T(8,128)(2,1)S(1)}, bf16[128,2048]{1,0:T(8,128)(2,1)}, u32[]{:S(2)}) copy-start(bf16[128,2048]{1,0:T(8,128)(2,1)} %reduce-scatter.3.cloned.1.call-done) | copy-start | bytes 1572868
Sparse Core Ops, SparseCore 0:
  9.7 54.5 all-gather.2
  109.8 98.7 reduce-scatter.2
  212.1 50.8 all-gather.4
  431.9 97.2 reduce-scatter.4
where the time goes:
time: 547 us; the launch traced here: 538 us
  waiting for transfers between devices  250 us (46%)
  local copies, waits for them, and re-layouts  114 us (21%)
  other arithmetic  78.1 us (14%)
  matrix products  68 us (12%)
  between operations  14.4 us (3%)
  loops' own time  8.39 us (2%)
    reduce_scatter x1, waiting for transfers between devices, shards(): lax.psum_scatter(jnp.dot(context, output_weight, preferred_element_type=j...  98.4 us
    unnamed x35, local copies, waits for them, and re-layouts  92.6 us
    reduce_scatter x1, waiting for transfers between devices, shards(): lax.psum_scatter(term.astype(jnp.bfloat16), 'tensor', scatter_dimension=0...  91.4 us
    all_gather x1, waiting for transfers between devices, shards(): lax.all_gather(tokens, 'tensor', axis=0, tiled=True)  56.3 us
    scatter-add x1, other arithmetic, shards(): term = term.at[stream_slots].add(weighted)  26.5 us
    another operation x1, other arithmetic, slot_tables(): before = jnp.cumsum(hits, axis=0) - hits  23.3 us
    dot_general x1, matrix products, expert_apply(): jnp.einsum('secf,efd->secd', hidden, expert_down, preferred_element_type=...  21 us
    dot_general x1, matrix products, expert_apply(): jnp.einsum('secd,edf->secf', incoming, expert_up, preferred_element_type=...  11.7 us
  transfers between devices with their start and end apart: 5, of which 4 were waited for; matrix products, arithmetic and copies ran while one was open for 31% of the time, Pallas kernels for 0%

commit v1 on v0

--- a/solution.py
+++ b/solution.py
@@ -98,7 +98,13 @@
     head_count = inner // HD
     projection = jnp.concatenate([query_weight, key_weight, value_weight], axis=1)
     projected = jnp.dot(
-        rms_scale(lax.all_gather(tokens, "tensor", axis=0, tiled=True), attention_gain),
+        rms_scale(
+            jnp.concatenate(
+                lax.all_to_all(jnp.stack([tokens] * lax.axis_size("tensor")), "tensor", 0, 0),
+                axis=0,
+            ),
+            attention_gain,
+        ),
         projection,
         preferred_element_type=jnp.float32,
     ).astype(jnp.bfloat16)

time: 547 us -> 605 us (1.11)
  waiting for transfers between devices: 250 us -> 288 us
  other arithmetic: 78.1 us -> 86.6 us
    all_to_all x0 -> x1, waiting for transfers between devices: none -> 95.3 us  [shards(): lax.all_to_all(jnp.stack([tokens] * lax.axis_size('tensor')), 'tensor', 0...]
    all_gather x1 -> x0, waiting for transfers between devices: 56.3 us -> none  [shards(): lax.all_gather(tokens, 'tensor', axis=0, tiled=True)]
    convert_element_type x1 -> x2, other arithmetic: 2.04 us -> 10.7 us  [rms_scale(): return (widened * inverse * gain).astype(jnp.bfloat16)]
    unnamed x35 -> x37, local copies, waits for them, and re-layouts: 92.6 us -> 92.1 us
  transfers between devices with their start and end apart: 5 -> 5, of which waited for: 4 -> 4; matrix products, arithmetic and copies ran while one was open for 31% -> 28% of each run, Pallas kernels for 0% -> 0%
where the time goes in v1:
time: 605 us; the launch traced here: 597 us
  waiting for transfers between devices  288 us (48%)
  local copies, waits for them, and re-layouts  119 us (20%)
  other arithmetic  86.6 us (14%)
  matrix products  69.9 us (12%)
  between operations  14.4 us (2%)
  starting transfers between devices  10.4 us (2%)
  loops' own time  8.84 us (1%)
    reduce_scatter x1, waiting for transfers between devices, shards(): lax.psum_scatter(jnp.dot(context, output_weight, preferred_element_type=j...  98.3 us
    all_to_all x1, waiting for transfers between devices, shards(): lax.all_to_all(jnp.stack([tokens] * lax.axis_size('tensor')), 'tensor', 0...  95.3 us
    unnamed x37, local copies, waits for them, and re-layouts  92.1 us
    reduce_scatter x1, waiting for transfers between devices, shards(): lax.psum_scatter(term.astype(jnp.bfloat16), 'tensor', scatter_dimension=0...  91.4 us
    scatter-add x1, other arithmetic, shards(): term = term.at[stream_slots].add(weighted)  26.5 us
    another operation x1, other arithmetic, slot_tables(): before = jnp.cumsum(hits, axis=0) - hits  23.3 us
    dot_general x1, matrix products, expert_apply(): jnp.einsum('secf,efd->secd', hidden, expert_down, preferred_element_type=...  21 us
  transfers between devices with their start and end apart: 5, of which 4 were waited for; matrix products, arithmetic and copies ran while one was open for 28% of the time, Pallas kernels for 0%

profile of v1, /device:TPU:0, one launch (start us, length us, event | category | flops | bytes accessed | tf_op | source)
XLA Modules:
  0.0 597.1 jit_solution(14358364524825097592)
XLA Ops:
  7.2 5.4 stack.8
  12.6 5.6 all-to-all-start
  18.3 95.3 %all-to-all-done = bf16[16,128,2048]{2,1,0:T(8,128)(2,1)} async-done(((bf16[16,128,2048]{2,1,0:T(8,128)(2,1)}), bf16[16,128,2048]{2,1,0:T(8,128)(2,1)}, u32[]{:S(2)}, u32[]{:S(2)}) %all-to-all-start) | async-done | bytes 8388640 | tf_op jit(solution)/shard_map/all_to_all | solution.py:103
  113.6 5.1 multiply_reduce_fusion
  118.7 8.7 %fusion.14 = bf16[2048,2048]{1,0:T(8,128)(2,1)} fusion(f32[2048]{0:T(1024)S(1)} %copy-done.7, f32[2048]{0:T(1024)S(1)} %rsqrt_bitcast_fusion, bf16[16,128,2048]{2,1,0:T(8,128)(2,1)} %all-to-all-done), kind=kLoop, calls=%fused_computation.24 | loop fusion | flops 16777216 | bytes 16793600 | tf_op jit(solution)/shard_map/convert_element_type | solution.py:14
  127.4 7.9 %convolution_convert_fusion.1 = bf16[2048,384]{1,0:T(8,128)(2,1)S(1)} fusion(bf16[2048,2048]{1,0:T(8,128)(2,1)} %fusion.14, bf16[2048,128]{1,0:T(8,128)(2,1)S(1)} %copy-done.12, bf16[2048,128]{1,0:T(8,128)(2,1)S(1)} %copy-done.13, bf16[2048,128]{1,0:T(8,128)(2,1)S(1)} %copy-done.14), kind=kOutput, calls=%fused_computation.47 | convolution fusion | flops 3226730496 | bytes 11534336 | tf_op jit(solution)/shard_map/dot_general | solution.py:100
  136.5 26.2 %while.11 = (s32[]{:T(128)}, bf16[4,512,1,128]{3,1,2,0:T(8,128)(2,1)S(1)}, s32[4]{0:T(128)S(1)}, s32[2048]{0:T(1024)S(1)}, bf16[2048,1,128]{2,0,1:T(8,128)(2,1)S...) while((s32[]{:T(128)}, ...), condition=%wide.region_4.5_spmd.clone, body=%wide.region_1.4_spmd.clone.sunk | while | flops 548470272 | bytes 13922475 | solution.py:45
  162.7 6.6 %convolution_convert_fusion = bf16[2048,2048]{1,0:T(8,128)(2,1)} fusion(bf16[2048,128]{1,0:T(8,128)(2,1)S(1)} %bitcast.153, bf16[128,2048]{1,0:T(8,128)(2,1)} %param.25), kind=kOutput, calls=%fused_computation.28 | convolution fusion | flops 1077936128 | bytes 9437184 | tf_op jit(solution)/shard_map/dot_general | solution.py:115
  169.4 98.3 %reduce-scatter.3.cloned.1.call-done = bf16[128,2048]{1,0:T(8,128)(2,1)} async-done(((bf16[2048,2048]{1,0:T(8,128)(2,1)}), bf16[128,2048]{1,0:T(8,128)(2,1)}) %reduce-scatter.3.cloned.1.call-update) | async-done | bytes 524304 | tf_op jit(solution)/shard_map/reduce_scatter | solution.py:114
  274.9 23.3 %fusion.70 = s32[16,128,16]{2,0,1:T(8,128)S(1)} fusion(s32[16,128,16]{2,0,1:T(8,128)S(1)} %copy.43), kind=kOutput, calls=%fused_computation.103 | output fusion | flops 4161536 | bytes 262144 | tf_op jit(solution)/shard_map/vmap(jit(cumsum))/reduce_window_sum | solution.py:54
  301.8 45.4 %scatter_custom_fusion.2 = s32[16384]{0:T(1024)S(1)} fusion(s32[12288]{0:T(1024)S(1)} %reshape.290, s32[12288]{0:T(1024)S(1)} %reshape.292, s32[]{:T(128)} %constant.27.clone.1), kind=kCustom, calls=%fused_computation.80 | custom fusion | bytes 65540
  347.5 6.1 %gather_fusion = bf16[1024,2048]{1,0:T(8,128)(2,1)} fusion(bf16[128,2048]{1,0:T(8,128)(2,1)S(1)} %copy-done.1, s32[1024]{0:T(1024)S(1)} %broadcast_clamp_fusion), kind=kCustom, calls=%fused_computation | custom fusion | bytes 8392704 | tf_op jit(solution)/shard_map/gather | solution.py:151
  353.5 4.7 all-to-all-start.1
  359.5 45.6 %scatter_custom_fusion.3 = f32[16384]{0:T(1024)S(1)} fusion(s32[12288]{0:T(1024)S(1)} %reshape.290, f32[12288]{0:T(1024)S(1)} %reshape.298, f32[]{:T(128)} %constant.9.clone.1), kind=kCustom, calls=%fused_computation.78 | custom fusion | bytes 65540
  405.3 3.3 all-to-all-done.1
  408.6 11.7 %fusion.19 = f32[16,64,1408]{2,1,0:T(8,128)} fusion(bf16[1,2048,1408]{2,1,0:T(8,128)(2,1)} %param.31, bf16[16,1,64,2048]{3,2,1,0:T(8,128)(2,1)} %all-to-all-done.1), kind=kOutput, calls=%fused_computation.33 | convolution fusion | flops 5905580032 | bytes 15728640 | tf_op jit(solution)/shard_map/secd,edf->secf/dot_general | solution.py:69
  420.3 21.0 %fusion.31 = bf16[16,64,2048]{2,1,0:T(8,128)(2,1)} fusion(bf16[1,1408,2048]{2,1,0:T(8,128)(2,1)} %param.32, f32[16,64,1408]{2,1,0:T(8,128)} %fusion.19, bf16[1,2048,1408]{2,1,0:T(8,128)(2,1)} %param.30, bf16[16,1,64,2048]{3,2,1,0:T(8,128)(2,1)} %all-to-all-done.1), kind=kOutput, calls=%fused_computation.45 | convolution fusion | flops 11821907968 | bytes 25690112 | tf_op jit(solution)/shard_map/secf,efd->secd/dot_general | solution.py:71
  441.3 5.8 fusion.49
  447.1 8.1 %fusion.57 = f32[2048,2048]{1,0:T(8,128)} fusion(bf16[176,2048]{1,0:T(8,128)(2,1)S(1)} %copy-done, f32[2048,352]{0,1:T(8,128)S(1)} %fusion.49), kind=kOutput, calls=%fused_computation.71 | convolution fusion | flops 1478557696 | bytes 20381696 | tf_op jit(solution)/shard_map/dot_general | solution.py:158
  455.2 26.5 %scatter_custom_fusion = f32[2048,2048]{1,0:T(8,128)} fusion(f32[2048,2048]{1,0:T(8,128)} %fusion.57, s32[1024]{0:T(1024)S(1)} %bitcast.157, bf16[1024,2048]{1,0:T(8,128)(2,1)} %bitcast.150, f32[1024]{0:T(1024)S(1)} %mul.121), kind=kCustom, calls=%fused_computation.27 | custom fusion | flops 6291456 | bytes 20975616 | tf_op jit(solution)/shard_map/scatter-add | solution.py:161
  481.8 9.1 %convert_element_type.109 = bf16[2048,2048]{1,0:T(8,128)(2,1)} convert(f32[2048,2048]{1,0:T(8,128)} %scatter_custom_fusion) | non-fusion elementwise | flops 4194304 | bytes 25165824 | tf_op jit(solution)/shard_map/convert_element_type | solution.py:163
  493.9 3.0 scatter_fusion
  496.9 91.4 %reduce-scatter.5.cloned.1.call-done = bf16[128,2048]{1,0:T(8,128)(2,1)} async-done(((bf16[2048,2048]{1,0:T(8,128)(2,1)}), bf16[128,2048]{1,0:T(8,128)(2,1)}) %reduce-scatter.5.cloned.1.call-update) | async-done | bytes 524304 | tf_op jit(solution)/shard_map/reduce_scatter | solution.py:162
  588.3 2.1 fusion.56
  (108 shorter events, 34.1 us)
Async XLA Ops:
  7.2 439.9 %copy-start = (bf16[176,2048]{1,0:T(8,128)(2,1)S(1)}, bf16[176,2048]{1,0:T(8,128)(2,1)}, u32[]{:S(2)}) copy-start(bf16[176,2048]{1,0:T(8,128)(2,1)} %param.29) | copy-start | bytes 2162692
  12.6 101.0 %all-to-all-start = ((bf16[16,128,2048]{2,1,0:T(8,128)(2,1)}), bf16[16,128,2048]{2,1,0:T(8,128)(2,1)}, u32[]{:S(2)}, u32[]{:S(2)}) async-start(bf16[16,128,2048]{2,1,0:T(8,128)(2,1)} %stack.8), calls=%async_computation | async-start | bytes 16777216 | tf_op jit(solution)/shard_map/all_to_all | solution.py:103
  18.2 249.5 %reduce-scatter.3.cloned.1.call-start = ((), (), s32[]{:S(2)}) async-start(), calls=%async_computation.4 | async-start | bytes 8912896 | tf_op jit(solution)/shard_map/reduce_scatter | solution.py:114
  18.3 100.4 %copy-start.7 = (f32[2048]{0:T(1024)S(1)}, f32[2048]{0:T(1024)}, u32[]{:S(2)}) copy-start(f32[2048]{0:T(1024)} %param.21) | copy-start | bytes 24580
  118.7 8.7 %copy-start.12 = (bf16[2048,128]{1,0:T(8,128)(2,1)S(1)}, bf16[2048,128]{1,0:T(8,128)(2,1)}, u32[]{:S(2)}) copy-start(bf16[2048,128]{1,0:T(8,128)(2,1)} %param.24) | copy-start | bytes 1572868
  118.7 8.7 %copy-start.13 = (bf16[2048,128]{1,0:T(8,128)(2,1)S(1)}, bf16[2048,128]{1,0:T(8,128)(2,1)}, u32[]{:S(2)}) copy-start(bf16[2048,128]{1,0:T(8,128)(2,1)} %param.23) | copy-start | bytes 1572868
  118.7 8.7 %copy-start.14 = (bf16[2048,128]{1,0:T(8,128)(2,1)S(1)}, bf16[2048,128]{1,0:T(8,128)(2,1)}, u32[]{:S(2)}) copy-start(bf16[2048,128]{1,0:T(8,128)(2,1)} %param.22) | copy-start | bytes 1572868
  135.3 1.2 copy-start.6
  169.3 98.4 %copy-start.2 = (bf16[128,2048]{1,0:T(8,128)(2,1)S(1)}, bf16[128,2048]{1,0:T(8,128)(2,1)}, u32[]{:S(2)}) copy-start(bf16[128,2048]{1,0:T(8,128)(2,1)} %param.19) | copy-start | bytes 1572868
  169.3 99.7 %copy-start.8 = (f32[2048]{0:T(1024)S(1)}, f32[2048]{0:T(1024)}, u32[]{:S(2)}) copy-start(f32[2048]{0:T(1024)} %param.26) | copy-start | bytes 24580
  169.3 101.9 %copy-start.4 = (s32[2048,6]{0,1:T(8,128)S(1)}, s32[2048,6]{0,1:T(8,128)}, u32[]{:S(2)}) copy-start(s32[2048,6]{0,1:T(8,128)} %param.33) | copy-start | bytes 147460
  169.3 272.0 %all-gather.2.cloned.1.call-start = ((), (), s32[]{:S(2)}) async-start(), calls=%async_computation.5 | async-start | bytes 8912896 | tf_op jit(solution)/shard_map/all_gather | solution.py:143
  274.9 26.8 %copy-start.10 = (s32[2]{0:T(128)S(1)}, s32[2]{0:T(128)}, u32[]{:S(2)}) copy-start(s32[2]{0:T(128)} %constant.41) | copy-start | bytes 28
  274.9 26.8 %copy-start.9 = (s32[2]{0:T(128)S(1)}, s32[2]{0:T(128)}, u32[]{:S(2)}) copy-start(s32[2]{0:T(128)} %constant.69) | copy-start | bytes 28
  298.2 49.3 %copy-start.1 = (bf16[128,2048]{1,0:T(8,128)(2,1)S(1)}, bf16[128,2048]{1,0:T(8,128)(2,1)}, u32[]{:S(2)}) copy-start(bf16[128,2048]{1,0:T(8,128)(2,1)} %fusion.55) | copy-start | bytes 1572868
  353.5 4.9 copy-start.5
  353.5 55.0 %all-to-all-start.1 = ((bf16[16,1,64,2048]{3,2,1,0:T(8,128)(2,1)}), bf16[16,1,64,2048]{3,2,1,0:T(8,128)(2,1)}, u32[]{:S(2)}, u32[]{:S(2)}) async-start(bf16[16,1,64,2048]{3,2,1,0:T(8,128)(2,1)} %bitcast.149), calls=%async_computation.2 | async-start | bytes 8388608 | tf_op jit(solution)/shard_map/all_to_all | solution.py:153
  358.2 230.1 %reduce-scatter.5.cloned.1.call-start = ((), (), s32[]{:S(2)}) async-start(), calls=%async_computation.6 | async-start | bytes 8912896 | tf_op jit(solution)/shard_map/reduce_scatter | solution.py:162
  420.3 21.0 %copy-start.11 = (bf16[2048,176]{0,1:T(8,128)(2,1)S(1)}, bf16[2048,176]{0,1:T(8,128)(2,1)}, u32[]{:S(2)}) copy-start(bf16[2048,176]{0,1:T(8,128)(2,1)} %param.28) | copy-start | bytes 2162692
  490.8 0.7 copy-start.15
  491.5 96.8 %copy-start.3 = (bf16[128,2048]{1,0:T(8,128)(2,1)S(1)}, bf16[128,2048]{1,0:T(8,128)(2,1)}, u32[]{:S(2)}) copy-start(bf16[128,2048]{1,0:T(8,128)(2,1)} %reduce-scatter.3.cloned.1.call-done) | copy-start | bytes 1572868
Sparse Core Ops, SparseCore 0:
  169.4 98.1 reduce-scatter.2
  271.2 50.8 all-gather.1
  491.0 97.2 reduce-scatter.4
